TPU v7x, 256 devices: a whole 4x4x8 slice. The times are simulated.
256 devices in a mesh: seq: 16 (over y, z_hi, core), head: 16 (over x, z_lo).
Axes of the slice: x: 4, y: 4, z: 8 (z_hi: 2, z_lo: 4; z = z_hi * 4 + z_lo), core: 2. Of those that a mesh axis runs over, the one named last changes fastest.
Arguments:
- x_in: bfloat16 [8192, 8192], P('seq', 'head'), may hold values from -6 to 6
- z_in: bfloat16 [8192, 8192], P('seq', 'head'), may hold values from -12 to 12
- bc: bfloat16 [2, 8192, 128], P(None, 'seq'), may hold values from -1.796875 to 1.796875
- dt_raw: float32 [128, 8192], P('head', 'seq'), may hold values from -3 to 3
- dt_bias: float32 [128], P('head'), may hold values from -8 to 0
- decay_rate: float32 [128], P('head'), may hold values from 0.001 to 0.4
- d_skip: float32 [128], P('head'), may hold values from 0.5 to 1.5
- norm_gain: float32 [8192], P('head'), may hold values from 0.1 to 1.9
- out_weight: bfloat16 [8192, 4096], P('head', 'seq'), may hold values from -0.0625 to 0.0625
- resid: bfloat16 [8192, 4096], P(('seq', 'head')), may hold values from -6 to 6
- mlp_gain: float32 [4096], replicated, may hold values from 0.1 to 1.9
- gate_weight: bfloat16 [4096, 8192], P(None, 'head'), may hold values from -0.09375 to 0.09375
- up_weight: bfloat16 [4096, 8192], P(None, 'head'), may hold values from -0.09375 to 0.09375
- down_weight: bfloat16 [8192, 4096], P('head', 'seq'), may hold values from -0.0625 to 0.0625
Outputs:
- layer_out: bfloat16 [8192, 4096], P(('seq', 'head'))
All inputs are finite; a program needn't handle non-finite values.
Results may differ from a plain program's by a relative error of at most 0.0075.
Values may be sent and summed in bfloat16 or wider, within the bound.
No kernel may reach another device: no remote copies, remote signals or barrier semaphores. Data moves between devices by JAX's collectives and lax.ppermute only.
A program may use at most 128 MiB of HBM per device.

v0:
```python
import jax
import jax.numpy as jnp
from jax import lax
from jax.sharding import PartitionSpec as P

BLOCK = 256
INNER = 8192
epsilon = 1e-05


def passed_along(value, axis, steps):
    count = lax.axis_size(axis)
    initial, last = (max(0, -steps), min(count, count - steps))
    return lax.ppermute(value, axis, [(source, source + steps) for source in range(initial, last)])


def block_scan(x_heads, b_rows, c_rows, step_size, log_decay, block_len, start_state):
    length, head_count, head_width = x_heads.shape
    state_size = b_rows.shape[1]
    block_count = length // block_len
    x_blocks = x_heads.reshape(block_count, block_len, head_count, head_width)
    b_blocks = b_rows.reshape(block_count, block_len, state_size)
    c_blocks = c_rows.reshape(block_count, block_len, state_size)
    d_blocks = step_size.reshape(head_count, block_count, block_len).transpose(1, 0, 2)
    a_blocks = log_decay.reshape(head_count, block_count, block_len).transpose(1, 0, 2)
    lower_mask = jnp.tril(jnp.ones((block_len, block_len), dtype=bool))

    def advance(carry_state, inputs):
        x_block, b_block, c_block, d_block, a_block = inputs
        cumulative = jnp.cumsum(a_block, axis=1)
        gap_values = jnp.where(
            lower_mask[None], cumulative[:, :, None] - cumulative[:, None, :], -jnp.inf
        )
        scores = jnp.dot(c_block, b_block.T, preferred_element_type=jnp.float32)
        mixing = (jnp.exp(gap_values) * scores[None] * d_block[:, None, :]).astype(jnp.bfloat16)
        within = jnp.einsum("hij,jhp->ihp", mixing, x_block, preferred_element_type=jnp.float32)
        carried = jnp.einsum(
            "in,hpn->ihp", c_block.astype(jnp.float32), carry_state, precision=lax.Precision.HIGHEST
        )
        carried = carried * jnp.exp(cumulative).T[:, :, None]
        last_cum = cumulative[:, -1:]
        inject = (
            (jnp.exp(last_cum - cumulative) * d_block)[:, :, None]
            * b_block.astype(jnp.float32)[None]
        ).astype(jnp.bfloat16)
        added = jnp.einsum("jhp,hjn->hpn", x_block, inject, preferred_element_type=jnp.float32)
        new_state = jnp.exp(last_cum)[:, :, None] * carry_state + added
        return (new_state, within + carried)

    final_state, block_outs = lax.scan(
        advance, start_state, (x_blocks, b_blocks, c_blocks, d_blocks, a_blocks)
    )
    return (block_outs.reshape(length, head_count, head_width), final_state)


def normalize_rows(layer_sum, mlp_gain):
    mean_square = jnp.mean(layer_sum * layer_sum, axis=1, keepdims=True)
    return (layer_sum * lax.rsqrt(mean_square + epsilon) * mlp_gain).astype(jnp.bfloat16)


def shards(
    x_in,
    z_in,
    bc,
    dt_raw,
    dt_bias,
    decay_rate,
    d_skip,
    norm_gain,
    out_weight,
    resid,
    mlp_gain,
    gate_weight,
    up_weight,
    down_weight,
):
    out_full, down_full = (
        lax.all_gather(out_weight, "seq", axis=1, tiled=True),
        lax.all_gather(down_weight, "seq", axis=1, tiled=True),
    )
    head_count = dt_raw.shape[0]
    length = dt_raw.shape[1]
    head_width = x_in.shape[1] // head_count
    state_size = bc.shape[2]
    step_size = jax.nn.softplus(dt_raw + dt_bias[:, None])
    log_decay = -decay_rate[:, None] * step_size
    x_heads = x_in.reshape(length, head_count, head_width)
    zero_state = jnp.zeros((head_count, head_width, state_size), jnp.float32)
    local_out, local_state = block_scan(
        x_heads, bc[0], bc[1], step_size, log_decay, BLOCK, zero_state
    )
    running = jnp.cumsum(log_decay, axis=1)
    group_decay = jnp.exp(running[:, -1])

    def relay_step(relay_turn, incoming):
        outgoing = group_decay[:, None, None] * incoming + local_state
        return passed_along(outgoing, "seq", 1)

    entering = lax.fori_loop(0, lax.axis_size("seq") - 1, relay_step, zero_state)
    carried = jnp.einsum(
        "tn,hpn->thp", bc[1].astype(jnp.float32), entering, precision=lax.Precision.HIGHEST
    )
    carried = carried * jnp.exp(running).T[:, :, None]
    ssd_out = local_out + carried + d_skip[None, :, None] * x_heads.astype(jnp.float32)
    gated_out = ssd_out.reshape(length, head_count * head_width) * jax.nn.silu(
        z_in.astype(jnp.float32)
    )
    row_squares = jnp.sum(gated_out * gated_out, axis=1)
    gated_scaled = (gated_out * norm_gain).astype(jnp.bfloat16)
    partial_value = jnp.dot(gated_scaled, out_full, preferred_element_type=jnp.float32)
    part_rows, part_squares = (
        lax.psum_scatter(partial_value, "head", scatter_dimension=0, tiled=True),
        lax.psum_scatter(row_squares, "head", scatter_dimension=0, tiled=True),
    )
    layer_sum = (
        resid.astype(jnp.float32) + part_rows * lax.rsqrt(part_squares / INNER + epsilon)[:, None]
    )
    normed = normalize_rows(layer_sum, mlp_gain)
    rows_piece = lax.all_gather(normed, "head", axis=0, tiled=True)
    gate_part = jnp.dot(rows_piece, gate_weight, preferred_element_type=jnp.float32)
    up_part = jnp.dot(rows_piece, up_weight, preferred_element_type=jnp.float32)
    hidden = (jax.nn.silu(gate_part) * up_part).astype(jnp.bfloat16)
    rows_piece = hidden
    mlp_rows = lax.psum_scatter(
        jnp.dot(rows_piece, down_full, preferred_element_type=jnp.float32),
        "head",
        scatter_dimension=0,
        tiled=True,
    )
    return (layer_sum + mlp_rows).astype(jnp.bfloat16)


def solution(mesh):
    in_specs = (
        P("seq", "head"),
        P("seq", "head"),
        P(None, "seq", None),
        P("head", "seq"),
        P("head"),
        P("head"),
        P("head"),
        P("head"),
        P("head", "seq"),
        P(("seq", "head"), None),
        P(),
        P(None, "head"),
        P(None, "head"),
        P("head", "seq"),
    )
    out_specs = P(("seq", "head"), None)
    return jax.shard_map(shards, mesh=mesh, in_specs=in_specs, out_specs=out_specs, check_vma=False)
```

profile of v0, /device:TPU:1, one launch (start us, length us, event | category | flops | bytes accessed | tf_op | source)
XLA Modules:
  0.0 857.0 jit_solution(15409193931064395106)
XLA Ops:
  8.6 1.6 reshape.124
  14.6 30.4 %while.24 = (s32[]{:T(128)}, f32[8,64,128]{2,1,0:T(8,128)S(1)}, f32[2,256,8,64]{1,0,3,2:T(2,128)}, f32[2,8,256]{2,1,0:T(8,128)S(1)}, bf16[2,256,8,64]{1,3,2,0:T(...) while((s32[]{:T(128)}, f32[8,64,128]{2,1,0:T(8,128)S(1)}, ...), condition=%wide.region_3.4_spmd.clone, body=%wide.region_0.3_spmd.clone.sunk | while | flops 322801696 | bytes 6293764 | solution.py:50
  18.3 11.6 %dynamic_update_slice.6 = f32[2,256,8,64]{1,0,3,2:T(2,128)} dynamic-update-slice(f32[2,256,8,64]{1,0,3,2:T(2,128)} %get-tuple-element.266, f32[1,256,8,64]{1,0,3,2:T(1,128)S(1)} %copy.49, s32[]{:T(128)S(6)} %copy.54, s32[]{:T(128)} %constant.46.clone.1..sunk, s32[]{:T(128)} %constant.46.clone.1..sunk, s32[]{:T(128)} %constant.46.clone.1..sunk) | dynamic-update-slice | bytes 1048580 | tf_op jit(solution)/shard_map/while/body/jit(dynamic_update_index_in_dim)/dynamic_update_slice | solution.py:50
  33.5 11.5 %dynamic_update_slice.6 = f32[2,256,8,64]{1,0,3,2:T(2,128)} dynamic-update-slice(f32[2,256,8,64]{1,0,3,2:T(2,128)} %get-tuple-element.266, f32[1,256,8,64]{1,0,3,2:T(1,128)S(1)} %copy.49, s32[]{:T(128)S(6)} %copy.54, s32[]{:T(128)} %constant.46.clone.1..sunk, s32[]{:T(128)} %constant.46.clone.1..sunk, s32[]{:T(128)} %constant.46.clone.1..sunk) | dynamic-update-slice | bytes 1048580 | tf_op jit(solution)/shard_map/while/body/jit(dynamic_update_index_in_dim)/dynamic_update_slice | solution.py:50
  45.0 2.1 reshape.115
  47.4 212.9 %while.23 = (s32[]{:T(128)}, f32[8,64,128]{2,1,0:T(8,128)S(1)}, f32[8]{0:T(128)S(1)}, f32[8,64,128]{2,1,0:T(8,128)S(1)}, s32[]{:T(128)}) while((s32[]{:T(128)}, f32[8,64,128]{2,1,0:T(8,128)S(1)}, f32[8]{0:T(128)S(1)}, f32[8,64,128]{2,1,0:T(8,128)S(1)}, s32[]{:T(128)}) %tuple.53), condition=%wide.region_7.8_spmd, body=%wide.region_6.7_spmd.sunk | while | flops 131074 | bytes 1835141 | solution.py:99
  47.5 10.3 %collective-permute-start = (f32[8,64,128]{2,1,0:T(8,128)S(1)}, f32[8,64,128]{2,1,0:T(8,128)S(1)}, u32[]{:S(2)}, u32[]{:S(2)}) collective-permute-start(f32[8,64,128]{2,1,0:T(8,128)S(1)} %multiply_add_fusion.3), channel_id=1, source_target_pairs={{0,16},{16,32},{32,48},{48,64},{64,80},{80,96},{96,112},{112,128},... | collective-permute-start | bytes 786440 | tf_op jit(solution)/shard_map/while/body/eval_jaxpr/ppermute | solution.py:14
  57.9 12.1 %collective-permute-done = f32[8,64,128]{2,1,0:T(8,128)S(1)} collective-permute-done((f32[8,64,128]{2,1,0:T(8,128)S(1)}, f32[8,64,128]{2,1,0:T(8,128)S(1)}, u32[]{:S(2)}, u32[]{:S(2)}) %collective-permute-start) | collective-permute-done | bytes 262176 | tf_op jit(solution)/shard_map/while/body/eval_jaxpr/ppermute | solution.py:14
  70.0 10.5 %collective-permute-start = (f32[8,64,128]{2,1,0:T(8,128)S(1)}, f32[8,64,128]{2,1,0:T(8,128)S(1)}, u32[]{:S(2)}, u32[]{:S(2)}) collective-permute-start(f32[8,64,128]{2,1,0:T(8,128)S(1)} %multiply_add_fusion.3), channel_id=1, source_target_pairs={{0,16},{16,32},{32,48},{48,64},{64,80},{80,96},{96,112},{112,128},... | collective-permute-start | bytes 786440 | tf_op jit(solution)/shard_map/while/body/eval_jaxpr/ppermute | solution.py:14
  80.6 3.9 collective-permute-done
  84.5 8.4 collective-permute-start
  92.9 3.3 collective-permute-done
  96.3 8.3 collective-permute-start
  104.6 3.3 collective-permute-done
  108.0 8.3 collective-permute-start
  116.3 3.3 collective-permute-done
  119.7 8.3 collective-permute-start
  128.0 3.3 collective-permute-done
  131.4 8.3 collective-permute-start
  139.7 5.2 collective-permute-done
  145.0 8.4 collective-permute-start
  153.4 6.1 collective-permute-done
  159.6 8.4 collective-permute-start
  168.0 5.9 collective-permute-done
  174.0 8.4 collective-permute-start
  182.4 5.4 collective-permute-done
  187.9 8.4 collective-permute-start
  196.3 6.0 collective-permute-done
  202.4 8.4 collective-permute-start
  210.8 6.0 collective-permute-done
  216.9 8.4 collective-permute-start
  225.3 6.0 collective-permute-done
  231.4 8.4 collective-permute-start
  239.8 6.0 collective-permute-done
  245.9 8.4 collective-permute-start
  254.3 6.0 collective-permute-done
  260.3 2.5 fusion.34
  262.8 1.6 copy.39
  264.5 7.8 fusion.41
  274.6 40.6 %all-reduce = f32[512]{0:T(512)S(1)} all-reduce(f32[512]{0:T(512)S(1)} %multiply_reduce_fusion), channel_id=3, replica_groups=mesh['seq'=16,'head'=16] {'head'}, use_global_device_ids=true, to_apply=%region_10.11.clone | all-reduce | flops 512 | bytes 4096
  315.4 157.3 %reduce-scatter.3.cloned.1.call-done = f32[32,4096]{1,0:T(8,128)} async-done(((f32[512,4096]{1,0:T(8,128)}), f32[32,4096]{1,0:T(8,128)}) %reduce-scatter.3.cloned.1.call-update) | async-done | bytes 524304 | tf_op jit(solution)/shard_map/reduce_scatter | solution.py:112
  474.0 1.9 multiply_convert_fusion.6
  476.8 99.1 %all-gather.6.cloned.1.call-done = bf16[512,4096]{1,0:T(8,128)(2,1)} async-done(((bf16[32,4096]{1,0:T(8,128)(2,1)}), bf16[512,4096]{1,0:T(8,128)(2,1)}) %all-gather.6.cloned.1.call-update) | async-done | bytes 4194320 | tf_op jit(solution)/shard_map/all_gather | solution.py:119
  575.9 5.8 fusion.52
  581.7 72.2 %all-gather.8.cloned.1.call-done = bf16[512,4096]{1,0:T(8,128)(2,1)} async-done(((bf16[512,256]{1,0:T(8,128)(2,1)}), bf16[512,4096]{1,0:T(8,128)(2,1)}) %all-gather.8.cloned.1.call-update) | async-done | bytes 4194320 | tf_op jit(solution)/shard_map/all_gather | solution.py:79
  653.9 12.5 %fusion.40 = f32[512,4096]{1,0:T(8,128)} fusion(bf16[512,4096]{1,0:T(8,128)(2,1)} %all-gather.8.cloned.1.call-done, bf16[512,4096]{1,0:T(8,128)(2,1)} %all-gather.6.cloned.1.call-done, bf16[4096,512]{1,0:T(8,128)(2,1)} %param.30, f32[512,512]{1,0:T(8,128)S(1)} %fusion.52), kind=kOutput, calls=%fused_computation.61 | convolution fusion | flops 4296540160 | bytes 22020096 | tf_op jit(solution)/shard_map/dot_general | solution.py:125
  666.4 182.1 %reduce-scatter.5.cloned.1.call-done = f32[32,4096]{1,0:T(8,128)} async-done(((f32[512,4096]{1,0:T(8,128)}), f32[32,4096]{1,0:T(8,128)}) %reduce-scatter.5.cloned.1.call-update) | async-done | bytes 524304 | tf_op jit(solution)/shard_map/reduce_scatter | solution.py:124
  848.5 1.9 add_convert_fusion
  (89 shorter events, 19.1 us)
Async XLA Ops:
  6.5 257.9 %all-gather.4.cloned.1.call-start = ((), (), s32[]{:S(2)}) async-start(), calls=%async_computation.2 | async-start | bytes 4456448 | tf_op jit(solution)/shard_map/all_gather | solution.py:78
  7.3 465.5 %reduce-scatter.3.cloned.1.call-start = ((), (), s32[]{:S(2)}) async-start(), calls=%async_computation.3 | async-start | bytes 8912896 | tf_op jit(solution)/shard_map/reduce_scatter | solution.py:112
  45.0 215.3 %copy-start.5 = (f32[8]{0:T(128)S(1)}, f32[8]{0:T(128)}, u32[]{:S(2)}) copy-start(f32[8]{0:T(128)} %param.24) | copy-start | bytes 100
  47.4 217.1 %copy-start.2 = (bf16[512,512]{1,0:T(8,128)(2,1)S(1)}, bf16[512,512]{1,0:T(8,128)(2,1)}, u32[]{:S(2)}) copy-start(bf16[512,512]{1,0:T(8,128)(2,1)} %param.19) | copy-start | bytes 1572868
  47.4 217.1 %copy-start.3 = (f32[512]{0:T(512)S(1)}, f32[512]{0:T(512)}, u32[]{:S(2)}) copy-start(f32[512]{0:T(512)} %param.25) | copy-start | bytes 6148
  47.5 22.4 %collective-permute-start = (f32[8,64,128]{2,1,0:T(8,128)S(1)}, f32[8,64,128]{2,1,0:T(8,128)S(1)}, u32[]{:S(2)}, u32[]{:S(2)}) collective-permute-start(f32[8,64,128]{2,1,0:T(8,128)S(1)} %multiply_add_fusion.3), channel_id=1, source_target_pairs={{0,16},{16,32},{32,48},{48,64},{64,80},{80,96},{96,112},{112,128},... | collective-permute-start | bytes 786440 | tf_op jit(solution)/shard_map/while/body/eval_jaxpr/ppermute | solution.py:14
  70.0 14.4 %collective-permute-start = (f32[8,64,128]{2,1,0:T(8,128)S(1)}, f32[8,64,128]{2,1,0:T(8,128)S(1)}, u32[]{:S(2)}, u32[]{:S(2)}) collective-permute-start(f32[8,64,128]{2,1,0:T(8,128)S(1)} %multiply_add_fusion.3), channel_id=1, source_target_pairs={{0,16},{16,32},{32,48},{48,64},{64,80},{80,96},{96,112},{112,128},... | collective-permute-start | bytes 786440 | tf_op jit(solution)/shard_map/while/body/eval_jaxpr/ppermute | solution.py:14
  84.5 11.7 %collective-permute-start = (f32[8,64,128]{2,1,0:T(8,128)S(1)}, f32[8,64,128]{2,1,0:T(8,128)S(1)}, u32[]{:S(2)}, u32[]{:S(2)}) collective-permute-start(f32[8,64,128]{2,1,0:T(8,128)S(1)} %multiply_add_fusion.3), channel_id=1, source_target_pairs={{0,16},{16,32},{32,48},{48,64},{64,80},{80,96},{96,112},{112,128},... | collective-permute-start | bytes 786440 | tf_op jit(solution)/shard_map/while/body/eval_jaxpr/ppermute | solution.py:14
  96.3 11.6 %collective-permute-start = (f32[8,64,128]{2,1,0:T(8,128)S(1)}, f32[8,64,128]{2,1,0:T(8,128)S(1)}, u32[]{:S(2)}, u32[]{:S(2)}) collective-permute-start(f32[8,64,128]{2,1,0:T(8,128)S(1)} %multiply_add_fusion.3), channel_id=1, source_target_pairs={{0,16},{16,32},{32,48},{48,64},{64,80},{80,96},{96,112},{112,128},... | collective-permute-start | bytes 786440 | tf_op jit(solution)/shard_map/while/body/eval_jaxpr/ppermute | solution.py:14
  108.0 11.6 %collective-permute-start = (f32[8,64,128]{2,1,0:T(8,128)S(1)}, f32[8,64,128]{2,1,0:T(8,128)S(1)}, u32[]{:S(2)}, u32[]{:S(2)}) collective-permute-start(f32[8,64,128]{2,1,0:T(8,128)S(1)} %multiply_add_fusion.3), channel_id=1, source_target_pairs={{0,16},{16,32},{32,48},{48,64},{64,80},{80,96},{96,112},{112,128},... | collective-permute-start | bytes 786440 | tf_op jit(solution)/shard_map/while/body/eval_jaxpr/ppermute | solution.py:14
  119.7 11.6 %collective-permute-start = (f32[8,64,128]{2,1,0:T(8,128)S(1)}, f32[8,64,128]{2,1,0:T(8,128)S(1)}, u32[]{:S(2)}, u32[]{:S(2)}) collective-permute-start(f32[8,64,128]{2,1,0:T(8,128)S(1)} %multiply_add_fusion.3), channel_id=1, source_target_pairs={{0,16},{16,32},{32,48},{48,64},{64,80},{80,96},{96,112},{112,128},... | collective-permute-start | bytes 786440 | tf_op jit(solution)/shard_map/while/body/eval_jaxpr/ppermute | solution.py:14
  131.4 13.5 %collective-permute-start = (f32[8,64,128]{2,1,0:T(8,128)S(1)}, f32[8,64,128]{2,1,0:T(8,128)S(1)}, u32[]{:S(2)}, u32[]{:S(2)}) collective-permute-start(f32[8,64,128]{2,1,0:T(8,128)S(1)} %multiply_add_fusion.3), channel_id=1, source_target_pairs={{0,16},{16,32},{32,48},{48,64},{64,80},{80,96},{96,112},{112,128},... | collective-permute-start | bytes 786440 | tf_op jit(solution)/shard_map/while/body/eval_jaxpr/ppermute | solution.py:14
  145.0 14.5 %collective-permute-start = (f32[8,64,128]{2,1,0:T(8,128)S(1)}, f32[8,64,128]{2,1,0:T(8,128)S(1)}, u32[]{:S(2)}, u32[]{:S(2)}) collective-permute-start(f32[8,64,128]{2,1,0:T(8,128)S(1)} %multiply_add_fusion.3), channel_id=1, source_target_pairs={{0,16},{16,32},{32,48},{48,64},{64,80},{80,96},{96,112},{112,128},... | collective-permute-start | bytes 786440 | tf_op jit(solution)/shard_map/while/body/eval_jaxpr/ppermute | solution.py:14
  159.6 14.3 %collective-permute-start = (f32[8,64,128]{2,1,0:T(8,128)S(1)}, f32[8,64,128]{2,1,0:T(8,128)S(1)}, u32[]{:S(2)}, u32[]{:S(2)}) collective-permute-start(f32[8,64,128]{2,1,0:T(8,128)S(1)} %multiply_add_fusion.3), channel_id=1, source_target_pairs={{0,16},{16,32},{32,48},{48,64},{64,80},{80,96},{96,112},{112,128},... | collective-permute-start | bytes 786440 | tf_op jit(solution)/shard_map/while/body/eval_jaxpr/ppermute | solution.py:14
  174.0 13.8 %collective-permute-start = (f32[8,64,128]{2,1,0:T(8,128)S(1)}, f32[8,64,128]{2,1,0:T(8,128)S(1)}, u32[]{:S(2)}, u32[]{:S(2)}) collective-permute-start(f32[8,64,128]{2,1,0:T(8,128)S(1)} %multiply_add_fusion.3), channel_id=1, source_target_pairs={{0,16},{16,32},{32,48},{48,64},{64,80},{80,96},{96,112},{112,128},... | collective-permute-start | bytes 786440 | tf_op jit(solution)/shard_map/while/body/eval_jaxpr/ppermute | solution.py:14
  187.9 14.4 %collective-permute-start = (f32[8,64,128]{2,1,0:T(8,128)S(1)}, f32[8,64,128]{2,1,0:T(8,128)S(1)}, u32[]{:S(2)}, u32[]{:S(2)}) collective-permute-start(f32[8,64,128]{2,1,0:T(8,128)S(1)} %multiply_add_fusion.3), channel_id=1, source_target_pairs={{0,16},{16,32},{32,48},{48,64},{64,80},{80,96},{96,112},{112,128},... | collective-permute-start | bytes 786440 | tf_op jit(solution)/shard_map/while/body/eval_jaxpr/ppermute | solution.py:14
  202.4 14.4 %collective-permute-start = (f32[8,64,128]{2,1,0:T(8,128)S(1)}, f32[8,64,128]{2,1,0:T(8,128)S(1)}, u32[]{:S(2)}, u32[]{:S(2)}) collective-permute-start(f32[8,64,128]{2,1,0:T(8,128)S(1)} %multiply_add_fusion.3), channel_id=1, source_target_pairs={{0,16},{16,32},{32,48},{48,64},{64,80},{80,96},{96,112},{112,128},... | collective-permute-start | bytes 786440 | tf_op jit(solution)/shard_map/while/body/eval_jaxpr/ppermute | solution.py:14
  216.9 14.4 %collective-permute-start = (f32[8,64,128]{2,1,0:T(8,128)S(1)}, f32[8,64,128]{2,1,0:T(8,128)S(1)}, u32[]{:S(2)}, u32[]{:S(2)}) collective-permute-start(f32[8,64,128]{2,1,0:T(8,128)S(1)} %multiply_add_fusion.3), channel_id=1, source_target_pairs={{0,16},{16,32},{32,48},{48,64},{64,80},{80,96},{96,112},{112,128},... | collective-permute-start | bytes 786440 | tf_op jit(solution)/shard_map/while/body/eval_jaxpr/ppermute | solution.py:14
  231.4 14.4 %collective-permute-start = (f32[8,64,128]{2,1,0:T(8,128)S(1)}, f32[8,64,128]{2,1,0:T(8,128)S(1)}, u32[]{:S(2)}, u32[]{:S(2)}) collective-permute-start(f32[8,64,128]{2,1,0:T(8,128)S(1)} %multiply_add_fusion.3), channel_id=1, source_target_pairs={{0,16},{16,32},{32,48},{48,64},{64,80},{80,96},{96,112},{112,128},... | collective-permute-start | bytes 786440 | tf_op jit(solution)/shard_map/while/body/eval_jaxpr/ppermute | solution.py:14
  245.9 14.4 %collective-permute-start = (f32[8,64,128]{2,1,0:T(8,128)S(1)}, f32[8,64,128]{2,1,0:T(8,128)S(1)}, u32[]{:S(2)}, u32[]{:S(2)}) collective-permute-start(f32[8,64,128]{2,1,0:T(8,128)S(1)} %multiply_add_fusion.3), channel_id=1, source_target_pairs={{0,16},{16,32},{32,48},{48,64},{64,80},{80,96},{96,112},{112,128},... | collective-permute-start | bytes 786440 | tf_op jit(solution)/shard_map/while/body/eval_jaxpr/ppermute | solution.py:14
  272.3 0.7 copy-start.6
  272.3 200.4 %copy-start.1 = (bf16[32,4096]{1,0:T(8,128)(2,1)S(1)}, bf16[32,4096]{1,0:T(8,128)(2,1)}, u32[]{:S(2)}) copy-start(bf16[32,4096]{1,0:T(8,128)(2,1)} %param.27) | copy-start | bytes 786436
  272.3 201.7 %copy-start.4 = (f32[4096]{0:T(1024)S(1)}, f32[4096]{0:T(1024)}, u32[]{:S(2)}) copy-start(f32[4096]{0:T(1024)} %param.28) | copy-start | bytes 49156
  272.3 303.6 %all-gather.6.cloned.1.call-start = ((), (), s32[]{:S(2)}) async-start(), calls=%async_computation.4 | async-start | bytes 4456448 | tf_op jit(solution)/shard_map/all_gather | solution.py:119
  476.0 177.9 %all-gather.8.cloned.1.call-start = ((), (), s32[]{:S(2)}) async-start(), calls=%async_computation.5 | async-start | bytes 4456448 | tf_op jit(solution)/shard_map/all_gather | solution.py:79
  476.6 372.0 %reduce-scatter.5.cloned.1.call-start = ((), (), s32[]{:S(2)}) async-start(), calls=%async_computation.6 | async-start | bytes 8912896 | tf_op jit(solution)/shard_map/reduce_scatter | solution.py:124
  666.4 182.1 %copy-start = (f32[32,4096]{1,0:T(8,128)S(1)}, f32[32,4096]{1,0:T(8,128)}, u32[]{:S(2)}) copy-start(f32[32,4096]{1,0:T(8,128)} %reduce-scatter.3.cloned.1.call-done) | copy-start | bytes 1572868
Sparse Core Ops, SparseCore 0:
  9.9 89.6 all-gather.3
  272.5 200.2 reduce-scatter.2
  476.1 99.7 all-gather.5
  578.3 75.5 all-gather.7
  666.5 181.9 reduce-scatter.4
where the time goes:
time: 859 us; the launch traced here: 857 us
  waiting for transfers between devices  594 us (69%)
  starting transfers between devices  130 us (15%)
  blocking collectives  40.6 us (5%)
  local copies, waits for them, and re-layouts  34.6 us (4%)
  matrix products  32.4 us (4%)
  between operations  13.9 us (2%)
  other arithmetic  11.3 us (1%)
    reduce_scatter x1, waiting for transfers between devices, shards(): lax.psum_scatter(jnp.dot(rows_piece, down_full, preferred_element_type=jn...  182 us
    reduce_scatter x1, waiting for transfers between devices, shards(): lax.psum_scatter(partial_value, 'head', scatter_dimension=0, tiled=True)  157 us
    ppermute x15, starting transfers between devices, passed_along(): lax.ppermute(value, axis, [(source, source + steps) for source in range(i...  130 us
    all_gather x1, waiting for transfers between devices, shards(): rows_piece = lax.all_gather(normed, 'head', axis=0, tiled=True)  99.1 us
    ppermute x15, waiting for transfers between devices, passed_along(): lax.ppermute(value, axis, [(source, source + steps) for source in range(i...  81.7 us
    all_gather x1, waiting for transfers between devices, shards(): lax.all_gather(down_weight, 'seq', axis=1, tiled=True)  72.2 us
    unnamed x1, blocking collectives  40.6 us
    dynamic_update_slice x4, local copies, waits for them, and re-layouts, block_scan(): lax.scan(advance, start_state, (x_blocks, b_blocks, c_blocks, d_blocks, a...  24.2 us
  transfers between devices with their start and end apart: 20, of which 19 were waited for; matrix products, arithmetic and copies ran while one was open for 6% of the time, Pallas kernels for 0%

commit v1 on v0

--- a/solution.py
+++ b/solution.py
@@ -116,7 +116,9 @@
         resid.astype(jnp.float32) + part_rows * lax.rsqrt(part_squares / INNER + epsilon)[:, None]
     )
     normed = normalize_rows(layer_sum, mlp_gain)
-    rows_piece = lax.all_gather(normed, "head", axis=0, tiled=True)
+    rows_piece = jnp.concatenate(
+        lax.all_to_all(jnp.stack([normed] * lax.axis_size("head")), "head", 0, 0), axis=0
+    )
     gate_part = jnp.dot(rows_piece, gate_weight, preferred_element_type=jnp.float32)
     up_part = jnp.dot(rows_piece, up_weight, preferred_element_type=jnp.float32)
     hidden = (jax.nn.silu(gate_part) * up_part).astype(jnp.bfloat16)

time: 859 us -> 822 us (0.957)
  waiting for transfers between devices: 594 us -> 548 us
    all_to_all x0 -> x1, waiting for transfers between devices: none -> 123 us  [shards(): lax.all_to_all(jnp.stack([normed] * lax.axis_size('head')), 'head', 0, 0)]
    all_gather x1 -> x0, waiting for transfers between devices: 99.1 us -> none  [shards(): rows_piece = lax.all_gather(normed, 'head', axis=0, tiled=True)]
    all_gather x1, waiting for transfers between devices: 72.2 us -> 0.02 us  [shards(): lax.all_gather(down_weight, 'seq', axis=1, tiled=True)]
  transfers between devices with their start and end apart: 20 -> 20, of which waited for: 19 -> 18; matrix products, arithmetic and copies ran while one was open for 6% -> 6% of each run, Pallas kernels for 0% -> 0%
where the time goes in v1:
time: 822 us; the launch traced here: 819 us
  waiting for transfers between devices  548 us (67%)
  starting transfers between devices  136 us (17%)
  blocking collectives  40.9 us (5%)
  local copies, waits for them, and re-layouts  37.1 us (5%)
  matrix products  32.4 us (4%)
  between operations  13.9 us (2%)
  other arithmetic  10.6 us (1%)
    reduce_scatter x1, waiting for transfers between devices, shards(): lax.psum_scatter(jnp.dot(rows_piece, down_full, preferred_element_type=jn...  184 us
    reduce_scatter x1, waiting for transfers between devices, shards(): lax.psum_scatter(partial_value, 'head', scatter_dimension=0, tiled=True)  157 us
    ppermute x15, starting transfers between devices, passed_along(): lax.ppermute(value, axis, [(source, source + steps) for source in range(i...  130 us
    all_to_all x1, waiting for transfers between devices, shards(): lax.all_to_all(jnp.stack([normed] * lax.axis_size('head')), 'head', 0, 0)  123 us
    ppermute x15, waiting for transfers between devices, passed_along(): lax.ppermute(value, axis, [(source, source + steps) for source in range(i...  81.7 us
    unnamed x1, blocking collectives  40.9 us
    dynamic_update_slice x4, local copies, waits for them, and re-layouts, block_scan(): lax.scan(advance, start_state, (x_blocks, b_blocks, c_blocks, d_blocks, a...  24.2 us
  transfers between devices with their start and end apart: 20, of which 18 were waited for; matrix products, arithmetic and copies ran while one was open for 6% of the time, Pallas kernels for 0%

profile of v1, /device:TPU:1, one launch (start us, length us, event | category | flops | bytes accessed | tf_op | source)
XLA Modules:
  0.0 819.3 jit_solution(8749871022875343573)
XLA Ops:
  8.6 1.6 reshape.130
  14.6 30.3 %while.24 = (s32[]{:T(128)}, f32[8,64,128]{2,1,0:T(8,128)S(1)}, f32[2,256,8,64]{1,0,3,2:T(2,128)}, f32[2,8,256]{2,1,0:T(8,128)S(1)}, bf16[2,256,8,64]{1,3,2,0:T(...) while((s32[]{:T(128)}, f32[8,64,128]{2,1,0:T(8,128)S(1)}, ...), condition=%wide.region_3.4_spmd.clone, body=%wide.region_0.3_spmd.clone.sunk | while | flops 322801696 | bytes 6293764 | solution.py:50
  18.3 11.6 %dynamic_update_slice.6 = f32[2,256,8,64]{1,0,3,2:T(2,128)} dynamic-update-slice(f32[2,256,8,64]{1,0,3,2:T(2,128)} %get-tuple-element.266, f32[1,256,8,64]{1,0,3,2:T(1,128)S(1)} %copy.49, s32[]{:T(128)S(6)} %copy.54, s32[]{:T(128)} %constant.46.clone.1..sunk, s32[]{:T(128)} %constant.46.clone.1..sunk, s32[]{:T(128)} %constant.46.clone.1..sunk) | dynamic-update-slice | bytes 1048580 | tf_op jit(solution)/shard_map/while/body/jit(dynamic_update_index_in_dim)/dynamic_update_slice | solution.py:50
  33.4 11.5 %dynamic_update_slice.6 = f32[2,256,8,64]{1,0,3,2:T(2,128)} dynamic-update-slice(f32[2,256,8,64]{1,0,3,2:T(2,128)} %get-tuple-element.266, f32[1,256,8,64]{1,0,3,2:T(1,128)S(1)} %copy.49, s32[]{:T(128)S(6)} %copy.54, s32[]{:T(128)} %constant.46.clone.1..sunk, s32[]{:T(128)} %constant.46.clone.1..sunk, s32[]{:T(128)} %constant.46.clone.1..sunk) | dynamic-update-slice | bytes 1048580 | tf_op jit(solution)/shard_map/while/body/jit(dynamic_update_index_in_dim)/dynamic_update_slice | solution.py:50
  45.0 2.1 reshape.120
  47.4 212.8 %while.23 = (s32[]{:T(128)}, f32[8,64,128]{2,1,0:T(8,128)S(1)}, f32[8]{0:T(128)S(1)}, f32[8,64,128]{2,1,0:T(8,128)S(1)}, s32[]{:T(128)}) while((s32[]{:T(128)}, f32[8,64,128]{2,1,0:T(8,128)S(1)}, f32[8]{0:T(128)S(1)}, f32[8,64,128]{2,1,0:T(8,128)S(1)}, s32[]{:T(128)}) %tuple.53), condition=%wide.region_7.8_spmd, body=%wide.region_6.7_spmd.sunk | while | flops 131074 | bytes 1835141 | solution.py:99
  47.5 10.3 %collective-permute-start = (f32[8,64,128]{2,1,0:T(8,128)S(1)}, f32[8,64,128]{2,1,0:T(8,128)S(1)}, u32[]{:S(2)}, u32[]{:S(2)}) collective-permute-start(f32[8,64,128]{2,1,0:T(8,128)S(1)} %multiply_add_fusion.3), channel_id=1, source_target_pairs={{0,16},{16,32},{32,48},{48,64},{64,80},{80,96},{96,112},{112,128},... | collective-permute-start | bytes 786440 | tf_op jit(solution)/shard_map/while/body/eval_jaxpr/ppermute | solution.py:14
  57.8 12.1 %collective-permute-done = f32[8,64,128]{2,1,0:T(8,128)S(1)} collective-permute-done((f32[8,64,128]{2,1,0:T(8,128)S(1)}, f32[8,64,128]{2,1,0:T(8,128)S(1)}, u32[]{:S(2)}, u32[]{:S(2)}) %collective-permute-start) | collective-permute-done | bytes 262176 | tf_op jit(solution)/shard_map/while/body/eval_jaxpr/ppermute | solution.py:14
  70.0 10.5 %collective-permute-start = (f32[8,64,128]{2,1,0:T(8,128)S(1)}, f32[8,64,128]{2,1,0:T(8,128)S(1)}, u32[]{:S(2)}, u32[]{:S(2)}) collective-permute-start(f32[8,64,128]{2,1,0:T(8,128)S(1)} %multiply_add_fusion.3), channel_id=1, source_target_pairs={{0,16},{16,32},{32,48},{48,64},{64,80},{80,96},{96,112},{112,128},... | collective-permute-start | bytes 786440 | tf_op jit(solution)/shard_map/while/body/eval_jaxpr/ppermute | solution.py:14
  80.5 3.9 collective-permute-done
  84.5 8.4 %collective-permute-start = (f32[8,64,128]{2,1,0:T(8,128)S(1)}, f32[8,64,128]{2,1,0:T(8,128)S(1)}, u32[]{:S(2)}, u32[]{:S(2)}) collective-permute-start(f32[8,64,128]{2,1,0:T(8,128)S(1)} %multiply_add_fusion.3), channel_id=1, source_target_pairs={{0,16},{16,32},{32,48},{48,64},{64,80},{80,96},{96,112},{112,128},... | collective-permute-start | bytes 786440 | tf_op jit(solution)/shard_map/while/body/eval_jaxpr/ppermute | solution.py:14
  92.9 3.3 collective-permute-done
  96.2 8.3 %collective-permute-start = (f32[8,64,128]{2,1,0:T(8,128)S(1)}, f32[8,64,128]{2,1,0:T(8,128)S(1)}, u32[]{:S(2)}, u32[]{:S(2)}) collective-permute-start(f32[8,64,128]{2,1,0:T(8,128)S(1)} %multiply_add_fusion.3), channel_id=1, source_target_pairs={{0,16},{16,32},{32,48},{48,64},{64,80},{80,96},{96,112},{112,128},... | collective-permute-start | bytes 786440 | tf_op jit(solution)/shard_map/while/body/eval_jaxpr/ppermute | solution.py:14
  104.6 3.3 collective-permute-done
  107.9 8.3 %collective-permute-start = (f32[8,64,128]{2,1,0:T(8,128)S(1)}, f32[8,64,128]{2,1,0:T(8,128)S(1)}, u32[]{:S(2)}, u32[]{:S(2)}) collective-permute-start(f32[8,64,128]{2,1,0:T(8,128)S(1)} %multiply_add_fusion.3), channel_id=1, source_target_pairs={{0,16},{16,32},{32,48},{48,64},{64,80},{80,96},{96,112},{112,128},... | collective-permute-start | bytes 786440 | tf_op jit(solution)/shard_map/while/body/eval_jaxpr/ppermute | solution.py:14
  116.3 3.3 collective-permute-done
  119.6 8.3 %collective-permute-start = (f32[8,64,128]{2,1,0:T(8,128)S(1)}, f32[8,64,128]{2,1,0:T(8,128)S(1)}, u32[]{:S(2)}, u32[]{:S(2)}) collective-permute-start(f32[8,64,128]{2,1,0:T(8,128)S(1)} %multiply_add_fusion.3), channel_id=1, source_target_pairs={{0,16},{16,32},{32,48},{48,64},{64,80},{80,96},{96,112},{112,128},... | collective-permute-start | bytes 786440 | tf_op jit(solution)/shard_map/while/body/eval_jaxpr/ppermute | solution.py:14
  127.9 3.3 collective-permute-done
  131.4 8.3 %collective-permute-start = (f32[8,64,128]{2,1,0:T(8,128)S(1)}, f32[8,64,128]{2,1,0:T(8,128)S(1)}, u32[]{:S(2)}, u32[]{:S(2)}) collective-permute-start(f32[8,64,128]{2,1,0:T(8,128)S(1)} %multiply_add_fusion.3), channel_id=1, source_target_pairs={{0,16},{16,32},{32,48},{48,64},{64,80},{80,96},{96,112},{112,128},... | collective-permute-start | bytes 786440 | tf_op jit(solution)/shard_map/while/body/eval_jaxpr/ppermute | solution.py:14
  139.7 5.2 collective-permute-done
  144.9 8.4 %collective-permute-start = (f32[8,64,128]{2,1,0:T(8,128)S(1)}, f32[8,64,128]{2,1,0:T(8,128)S(1)}, u32[]{:S(2)}, u32[]{:S(2)}) collective-permute-start(f32[8,64,128]{2,1,0:T(8,128)S(1)} %multiply_add_fusion.3), channel_id=1, source_target_pairs={{0,16},{16,32},{32,48},{48,64},{64,80},{80,96},{96,112},{112,128},... | collective-permute-start | bytes 786440 | tf_op jit(solution)/shard_map/while/body/eval_jaxpr/ppermute | solution.py:14
  153.4 6.1 collective-permute-done
  159.5 8.4 %collective-permute-start = (f32[8,64,128]{2,1,0:T(8,128)S(1)}, f32[8,64,128]{2,1,0:T(8,128)S(1)}, u32[]{:S(2)}, u32[]{:S(2)}) collective-permute-start(f32[8,64,128]{2,1,0:T(8,128)S(1)} %multiply_add_fusion.3), channel_id=1, source_target_pairs={{0,16},{16,32},{32,48},{48,64},{64,80},{80,96},{96,112},{112,128},... | collective-permute-start | bytes 786440 | tf_op jit(solution)/shard_map/while/body/eval_jaxpr/ppermute | solution.py:14
  167.9 5.9 collective-permute-done
  173.9 8.4 %collective-permute-start = (f32[8,64,128]{2,1,0:T(8,128)S(1)}, f32[8,64,128]{2,1,0:T(8,128)S(1)}, u32[]{:S(2)}, u32[]{:S(2)}) collective-permute-start(f32[8,64,128]{2,1,0:T(8,128)S(1)} %multiply_add_fusion.3), channel_id=1, source_target_pairs={{0,16},{16,32},{32,48},{48,64},{64,80},{80,96},{96,112},{112,128},... | collective-permute-start | bytes 786440 | tf_op jit(solution)/shard_map/while/body/eval_jaxpr/ppermute | solution.py:14
  182.4 5.4 collective-permute-done
  187.8 8.4 %collective-permute-start = (f32[8,64,128]{2,1,0:T(8,128)S(1)}, f32[8,64,128]{2,1,0:T(8,128)S(1)}, u32[]{:S(2)}, u32[]{:S(2)}) collective-permute-start(f32[8,64,128]{2,1,0:T(8,128)S(1)} %multiply_add_fusion.3), channel_id=1, source_target_pairs={{0,16},{16,32},{32,48},{48,64},{64,80},{80,96},{96,112},{112,128},... | collective-permute-start | bytes 786440 | tf_op jit(solution)/shard_map/while/body/eval_jaxpr/ppermute | solution.py:14
  196.2 6.0 collective-permute-done
  202.3 8.4 %collective-permute-start = (f32[8,64,128]{2,1,0:T(8,128)S(1)}, f32[8,64,128]{2,1,0:T(8,128)S(1)}, u32[]{:S(2)}, u32[]{:S(2)}) collective-permute-start(f32[8,64,128]{2,1,0:T(8,128)S(1)} %multiply_add_fusion.3), channel_id=1, source_target_pairs={{0,16},{16,32},{32,48},{48,64},{64,80},{80,96},{96,112},{112,128},... | collective-permute-start | bytes 786440 | tf_op jit(solution)/shard_map/while/body/eval_jaxpr/ppermute | solution.py:14
  210.7 6.0 collective-permute-done
  216.8 8.4 %collective-permute-start = (f32[8,64,128]{2,1,0:T(8,128)S(1)}, f32[8,64,128]{2,1,0:T(8,128)S(1)}, u32[]{:S(2)}, u32[]{:S(2)}) collective-permute-start(f32[8,64,128]{2,1,0:T(8,128)S(1)} %multiply_add_fusion.3), channel_id=1, source_target_pairs={{0,16},{16,32},{32,48},{48,64},{64,80},{80,96},{96,112},{112,128},... | collective-permute-start | bytes 786440 | tf_op jit(solution)/shard_map/while/body/eval_jaxpr/ppermute | solution.py:14
  225.2 6.0 collective-permute-done
  231.3 8.4 %collective-permute-start = (f32[8,64,128]{2,1,0:T(8,128)S(1)}, f32[8,64,128]{2,1,0:T(8,128)S(1)}, u32[]{:S(2)}, u32[]{:S(2)}) collective-permute-start(f32[8,64,128]{2,1,0:T(8,128)S(1)} %multiply_add_fusion.3), channel_id=1, source_target_pairs={{0,16},{16,32},{32,48},{48,64},{64,80},{80,96},{96,112},{112,128},... | collective-permute-start | bytes 786440 | tf_op jit(solution)/shard_map/while/body/eval_jaxpr/ppermute | solution.py:14
  239.7 6.0 collective-permute-done
  245.8 8.4 %collective-permute-start = (f32[8,64,128]{2,1,0:T(8,128)S(1)}, f32[8,64,128]{2,1,0:T(8,128)S(1)}, u32[]{:S(2)}, u32[]{:S(2)}) collective-permute-start(f32[8,64,128]{2,1,0:T(8,128)S(1)} %multiply_add_fusion.3), channel_id=1, source_target_pairs={{0,16},{16,32},{32,48},{48,64},{64,80},{80,96},{96,112},{112,128},... | collective-permute-start | bytes 786440 | tf_op jit(solution)/shard_map/while/body/eval_jaxpr/ppermute | solution.py:14
  254.2 6.0 collective-permute-done
  260.2 2.5 fusion.34
  262.8 1.6 copy.39
  264.4 7.8 fusion.41
  274.6 40.9 %all-reduce = f32[512]{0:T(512)S(1)} all-reduce(f32[512]{0:T(512)S(1)} %multiply_reduce_fusion), channel_id=3, replica_groups=mesh['seq'=16,'head'=16] {'head'}, use_global_device_ids=true, to_apply=%region_10.11.clone | all-reduce | flops 512 | bytes 4096
  315.5 157.2 %reduce-scatter.3.cloned.1.call-done = f32[32,4096]{1,0:T(8,128)} async-done(((f32[512,4096]{1,0:T(8,128)}), f32[32,4096]{1,0:T(8,128)}) %reduce-scatter.3.cloned.1.call-update) | async-done | bytes 524304 | tf_op jit(solution)/shard_map/reduce_scatter | solution.py:112
  475.3 2.4 stack.2
  477.7 6.4 all-to-all-start
  485.1 123.4 %all-to-all-done = bf16[16,32,4096]{2,1,0:T(8,128)(2,1)} async-done(((bf16[16,32,4096]{2,1,0:T(8,128)(2,1)}), bf16[16,32,4096]{2,1,0:T(8,128)(2,1)}, u32[]{:S(2)}, u32[]{:S(2)}) %all-to-all-start) | async-done | bytes 4194336 | tf_op jit(solution)/shard_map/all_to_all | solution.py:120
  608.6 5.8 fusion.52
  614.4 12.5 %fusion.40 = f32[512,4096]{1,0:T(8,128)} fusion(bf16[512,4096]{1,0:T(8,128)(2,1)} %all-gather.5.cloned.1.call-done, bf16[512,4096]{1,0:T(8,128)(2,1)} %bitcast.14, bf16[4096,512]{1,0:T(8,128)(2,1)} %param.30, f32[512,512]{1,0:T(8,128)S(1)} %fusion.52), kind=kOutput, calls=%fused_computation.61 | convolution fusion | flops 4296540160 | bytes 22020096 | tf_op jit(solution)/shard_map/dot_general | solution.py:127
  626.9 183.9 %reduce-scatter.5.cloned.1.call-done = f32[32,4096]{1,0:T(8,128)} async-done(((f32[512,4096]{1,0:T(8,128)}), f32[32,4096]{1,0:T(8,128)}) %reduce-scatter.5.cloned.1.call-update) | async-done | bytes 524304 | tf_op jit(solution)/shard_map/reduce_scatter | solution.py:126
  810.9 1.9 add_convert_fusion
  (89 shorter events, 20.5 us)
Async XLA Ops:
  6.5 257.8 %all-gather.3.cloned.1.call-start = ((), (), s32[]{:S(2)}) async-start(), calls=%async_computation.3 | async-start | bytes 4456448 | tf_op jit(solution)/shard_map/all_gather | solution.py:78
  7.3 465.5 %reduce-scatter.3.cloned.1.call-start = ((), (), s32[]{:S(2)}) async-start(), calls=%async_computation.4 | async-start | bytes 8912896 | tf_op jit(solution)/shard_map/reduce_scatter | solution.py:112
  45.0 215.2 %copy-start.5 = (f32[8]{0:T(128)S(1)}, f32[8]{0:T(128)}, u32[]{:S(2)}) copy-start(f32[8]{0:T(128)} %param.24) | copy-start | bytes 100
  47.4 217.0 %copy-start.2 = (bf16[512,512]{1,0:T(8,128)(2,1)S(1)}, bf16[512,512]{1,0:T(8,128)(2,1)}, u32[]{:S(2)}) copy-start(bf16[512,512]{1,0:T(8,128)(2,1)} %param.19) | copy-start | bytes 1572868
  47.4 217.0 %copy-start.3 = (f32[512]{0:T(512)S(1)}, f32[512]{0:T(512)}, u32[]{:S(2)}) copy-start(f32[512]{0:T(512)} %param.25) | copy-start | bytes 6148
  47.5 22.4 %collective-permute-start = (f32[8,64,128]{2,1,0:T(8,128)S(1)}, f32[8,64,128]{2,1,0:T(8,128)S(1)}, u32[]{:S(2)}, u32[]{:S(2)}) collective-permute-start(f32[8,64,128]{2,1,0:T(8,128)S(1)} %multiply_add_fusion.3), channel_id=1, source_target_pairs={{0,16},{16,32},{32,48},{48,64},{64,80},{80,96},{96,112},{112,128},... | collective-permute-start | bytes 786440 | tf_op jit(solution)/shard_map/while/body/eval_jaxpr/ppermute | solution.py:14
  70.0 14.4 %collective-permute-start = (f32[8,64,128]{2,1,0:T(8,128)S(1)}, f32[8,64,128]{2,1,0:T(8,128)S(1)}, u32[]{:S(2)}, u32[]{:S(2)}) collective-permute-start(f32[8,64,128]{2,1,0:T(8,128)S(1)} %multiply_add_fusion.3), channel_id=1, source_target_pairs={{0,16},{16,32},{32,48},{48,64},{64,80},{80,96},{96,112},{112,128},... | collective-permute-start | bytes 786440 | tf_op jit(solution)/shard_map/while/body/eval_jaxpr/ppermute | solution.py:14
  84.5 11.7 %collective-permute-start = (f32[8,64,128]{2,1,0:T(8,128)S(1)}, f32[8,64,128]{2,1,0:T(8,128)S(1)}, u32[]{:S(2)}, u32[]{:S(2)}) collective-permute-start(f32[8,64,128]{2,1,0:T(8,128)S(1)} %multiply_add_fusion.3), channel_id=1, source_target_pairs={{0,16},{16,32},{32,48},{48,64},{64,80},{80,96},{96,112},{112,128},... | collective-permute-start | bytes 786440 | tf_op jit(solution)/shard_map/while/body/eval_jaxpr/ppermute | solution.py:14
  96.2 11.6 %collective-permute-start = (f32[8,64,128]{2,1,0:T(8,128)S(1)}, f32[8,64,128]{2,1,0:T(8,128)S(1)}, u32[]{:S(2)}, u32[]{:S(2)}) collective-permute-start(f32[8,64,128]{2,1,0:T(8,128)S(1)} %multiply_add_fusion.3), channel_id=1, source_target_pairs={{0,16},{16,32},{32,48},{48,64},{64,80},{80,96},{96,112},{112,128},... | collective-permute-start | bytes 786440 | tf_op jit(solution)/shard_map/while/body/eval_jaxpr/ppermute | solution.py:14
  107.9 11.6 %collective-permute-start = (f32[8,64,128]{2,1,0:T(8,128)S(1)}, f32[8,64,128]{2,1,0:T(8,128)S(1)}, u32[]{:S(2)}, u32[]{:S(2)}) collective-permute-start(f32[8,64,128]{2,1,0:T(8,128)S(1)} %multiply_add_fusion.3), channel_id=1, source_target_pairs={{0,16},{16,32},{32,48},{48,64},{64,80},{80,96},{96,112},{112,128},... | collective-permute-start | bytes 786440 | tf_op jit(solution)/shard_map/while/body/eval_jaxpr/ppermute | solution.py:14
  119.6 11.6 %collective-permute-start = (f32[8,64,128]{2,1,0:T(8,128)S(1)}, f32[8,64,128]{2,1,0:T(8,128)S(1)}, u32[]{:S(2)}, u32[]{:S(2)}) collective-permute-start(f32[8,64,128]{2,1,0:T(8,128)S(1)} %multiply_add_fusion.3), channel_id=1, source_target_pairs={{0,16},{16,32},{32,48},{48,64},{64,80},{80,96},{96,112},{112,128},... | collective-permute-start | bytes 786440 | tf_op jit(solution)/shard_map/while/body/eval_jaxpr/ppermute | solution.py:14
  131.4 13.5 %collective-permute-start = (f32[8,64,128]{2,1,0:T(8,128)S(1)}, f32[8,64,128]{2,1,0:T(8,128)S(1)}, u32[]{:S(2)}, u32[]{:S(2)}) collective-permute-start(f32[8,64,128]{2,1,0:T(8,128)S(1)} %multiply_add_fusion.3), channel_id=1, source_target_pairs={{0,16},{16,32},{32,48},{48,64},{64,80},{80,96},{96,112},{112,128},... | collective-permute-start | bytes 786440 | tf_op jit(solution)/shard_map/while/body/eval_jaxpr/ppermute | solution.py:14
  144.9 14.5 %collective-permute-start = (f32[8,64,128]{2,1,0:T(8,128)S(1)}, f32[8,64,128]{2,1,0:T(8,128)S(1)}, u32[]{:S(2)}, u32[]{:S(2)}) collective-permute-start(f32[8,64,128]{2,1,0:T(8,128)S(1)} %multiply_add_fusion.3), channel_id=1, source_target_pairs={{0,16},{16,32},{32,48},{48,64},{64,80},{80,96},{96,112},{112,128},... | collective-permute-start | bytes 786440 | tf_op jit(solution)/shard_map/while/body/eval_jaxpr/ppermute | solution.py:14
  159.5 14.3 %collective-permute-start = (f32[8,64,128]{2,1,0:T(8,128)S(1)}, f32[8,64,128]{2,1,0:T(8,128)S(1)}, u32[]{:S(2)}, u32[]{:S(2)}) collective-permute-start(f32[8,64,128]{2,1,0:T(8,128)S(1)} %multiply_add_fusion.3), channel_id=1, source_target_pairs={{0,16},{16,32},{32,48},{48,64},{64,80},{80,96},{96,112},{112,128},... | collective-permute-start | bytes 786440 | tf_op jit(solution)/shard_map/while/body/eval_jaxpr/ppermute | solution.py:14
  173.9 13.8 %collective-permute-start = (f32[8,64,128]{2,1,0:T(8,128)S(1)}, f32[8,64,128]{2,1,0:T(8,128)S(1)}, u32[]{:S(2)}, u32[]{:S(2)}) collective-permute-start(f32[8,64,128]{2,1,0:T(8,128)S(1)} %multiply_add_fusion.3), channel_id=1, source_target_pairs={{0,16},{16,32},{32,48},{48,64},{64,80},{80,96},{96,112},{112,128},... | collective-permute-start | bytes 786440 | tf_op jit(solution)/shard_map/while/body/eval_jaxpr/ppermute | solution.py:14
  187.8 14.4 %collective-permute-start = (f32[8,64,128]{2,1,0:T(8,128)S(1)}, f32[8,64,128]{2,1,0:T(8,128)S(1)}, u32[]{:S(2)}, u32[]{:S(2)}) collective-permute-start(f32[8,64,128]{2,1,0:T(8,128)S(1)} %multiply_add_fusion.3), channel_id=1, source_target_pairs={{0,16},{16,32},{32,48},{48,64},{64,80},{80,96},{96,112},{112,128},... | collective-permute-start | bytes 786440 | tf_op jit(solution)/shard_map/while/body/eval_jaxpr/ppermute | solution.py:14
  202.3 14.4 %collective-permute-start = (f32[8,64,128]{2,1,0:T(8,128)S(1)}, f32[8,64,128]{2,1,0:T(8,128)S(1)}, u32[]{:S(2)}, u32[]{:S(2)}) collective-permute-start(f32[8,64,128]{2,1,0:T(8,128)S(1)} %multiply_add_fusion.3), channel_id=1, source_target_pairs={{0,16},{16,32},{32,48},{48,64},{64,80},{80,96},{96,112},{112,128},... | collective-permute-start | bytes 786440 | tf_op jit(solution)/shard_map/while/body/eval_jaxpr/ppermute | solution.py:14
  216.8 14.4 %collective-permute-start = (f32[8,64,128]{2,1,0:T(8,128)S(1)}, f32[8,64,128]{2,1,0:T(8,128)S(1)}, u32[]{:S(2)}, u32[]{:S(2)}) collective-permute-start(f32[8,64,128]{2,1,0:T(8,128)S(1)} %multiply_add_fusion.3), channel_id=1, source_target_pairs={{0,16},{16,32},{32,48},{48,64},{64,80},{80,96},{96,112},{112,128},... | collective-permute-start | bytes 786440 | tf_op jit(solution)/shard_map/while/body/eval_jaxpr/ppermute | solution.py:14
  231.3 14.4 %collective-permute-start = (f32[8,64,128]{2,1,0:T(8,128)S(1)}, f32[8,64,128]{2,1,0:T(8,128)S(1)}, u32[]{:S(2)}, u32[]{:S(2)}) collective-permute-start(f32[8,64,128]{2,1,0:T(8,128)S(1)} %multiply_add_fusion.3), channel_id=1, source_target_pairs={{0,16},{16,32},{32,48},{48,64},{64,80},{80,96},{96,112},{112,128},... | collective-permute-start | bytes 786440 | tf_op jit(solution)/shard_map/while/body/eval_jaxpr/ppermute | solution.py:14
  245.8 14.4 %collective-permute-start = (f32[8,64,128]{2,1,0:T(8,128)S(1)}, f32[8,64,128]{2,1,0:T(8,128)S(1)}, u32[]{:S(2)}, u32[]{:S(2)}) collective-permute-start(f32[8,64,128]{2,1,0:T(8,128)S(1)} %multiply_add_fusion.3), channel_id=1, source_target_pairs={{0,16},{16,32},{32,48},{48,64},{64,80},{80,96},{96,112},{112,128},... | collective-permute-start | bytes 786440 | tf_op jit(solution)/shard_map/while/body/eval_jaxpr/ppermute | solution.py:14
  272.2 0.7 copy-start.6
  272.2 200.5 %copy-start.1 = (bf16[32,4096]{1,0:T(8,128)(2,1)S(1)}, bf16[32,4096]{1,0:T(8,128)(2,1)}, u32[]{:S(2)}) copy-start(bf16[32,4096]{1,0:T(8,128)(2,1)} %param.27) | copy-start | bytes 786436
  272.2 201.8 %copy-start.4 = (f32[4096]{0:T(1024)S(1)}, f32[4096]{0:T(1024)}, u32[]{:S(2)}) copy-start(f32[4096]{0:T(1024)} %param.28) | copy-start | bytes 49156
  477.7 130.8 %all-to-all-start = ((bf16[16,32,4096]{2,1,0:T(8,128)(2,1)}), bf16[16,32,4096]{2,1,0:T(8,128)(2,1)}, u32[]{:S(2)}, u32[]{:S(2)}) async-start(bf16[16,32,4096]{2,1,0:T(8,128)(2,1)} %stack.2), calls=%async_computation.1 | async-start | bytes 8388608 | tf_op jit(solution)/shard_map/all_to_all | solution.py:120
  484.1 130.2 %all-gather.5.cloned.1.call-start = ((), (), s32[]{:S(2)}) async-start(), calls=%async_computation.5 | async-start | bytes 4456448 | tf_op jit(solution)/shard_map/all_gather | solution.py:79
  484.9 326.0 %reduce-scatter.5.cloned.1.call-start = ((), (), s32[]{:S(2)}) async-start(), calls=%async_computation.6 | async-start | bytes 8912896 | tf_op jit(solution)/shard_map/reduce_scatter | solution.py:126
  626.9 184.0 %copy-start = (f32[32,4096]{1,0:T(8,128)S(1)}, f32[32,4096]{1,0:T(8,128)}, u32[]{:S(2)}) copy-start(f32[32,4096]{1,0:T(8,128)} %reduce-scatter.3.cloned.1.call-done) | copy-start | bytes 1572868
Sparse Core Ops, SparseCore 0:
  9.9 89.6 all-gather.2
  272.4 200.3 reduce-scatter.2
  487.5 117.2 all-gather.4
  627.0 183.7 reduce-scatter.4
